TPU v7x, 32 devices: a whole 2x2x4 slice. The times are simulated.
32 devices in a mesh: species: 4 (over z), space: 8 (over y, x, core).
Axes of the slice: x: 2, y: 2, z: 4, core: 2. Of those that a mesh axis runs over, the one named last changes fastest.
Arguments:
- density: float32 [4, 32, 16, 32, 128], P('species', None, 'space'), may hold values from 0 to 2
- space_factor: float32 [16, 32, 128], P('space'), may hold values from 0.5 to 1
- diff_rate: float32 [4, 32], P('species'), may hold values from 0.02 to 0.08
- loss_inverse: float32 [4, 32, 32], P('species'), may hold values from 0 to 1, as said below
- chain_yield: float32 [4, 32], P('species'), may hold values from 0.25 to 0.95
- survival: float32 [4, 32], P('species'), may hold values from 0.6 to 1
- gamma_yield: float32 [4, 32], P('species'), may hold values from 0.1 to 1
- sky_weight: bfloat16 [8, 8, 64, 128], P('space'), may hold values from -0.75 to 0.75
- sky_blocks: int32 [8, 8], P('space'), may hold values from 0 to 383
Outputs:
- propagated: float32 [4, 32, 16, 32, 128], P('species', None, 'space')
- sky: float32 [384, 128], P('space')
Inputs may be any that keep to these rules, and one draw needn't show every extreme that they name: `loss_inverse`: each matrix is upper triangular with a diagonal of 0.5 to 1 and nonnegative entries.
All inputs are finite; a program needn't handle non-finite values.
Results may differ from a plain program's by a relative error of at most 0.0011.
Values sent between devices are 32-bit elements; how exact they have to be, the bound alone decides.
No kernel may reach another device: no remote copies, remote signals or barrier semaphores. Data moves between devices by JAX's collectives and lax.ppermute only.
A program may use at most 64 MiB of HBM per device.

v0:
```python
import jax
import jax.numpy as jnp
from jax import lax
from jax.sharding import PartitionSpec as P

SUBSTEPS = 2
NB = 384
HIGH = lax.Precision.HIGHEST


def padded_2(cells, sides, width):
    for axis, dim in sides:
        count = lax.axis_size(axis)
        ends = count - 1
        head = lax.slice_in_dim(cells, 0, width, axis=dim)
        tail = lax.slice_in_dim(cells, cells.shape[dim] - width, cells.shape[dim], axis=dim)
        cells = jnp.concatenate(
            [
                lax.ppermute(tail, axis, [(i, (i + 1) % count) for i in range(ends)]),
                cells,
                lax.ppermute(head, axis, [((i + 1) % count, i) for i in range(ends)]),
            ],
            axis=dim,
        )
    return cells


def from_behind(block, axis, distance):
    devices = range(lax.axis_size(axis))
    route = [(i - distance, i) for i in devices if i - distance in devices]
    return lax.ppermute(block, axis, route)


def cross_sum(field):
    padded = jnp.pad(field, ((0, 0), (0, 0), (1, 1), (1, 1)))
    beside = padded[:, :, 2:, 1:-1] + padded[:, :, :-2, 1:-1]
    beside = beside + padded[:, :, 1:-1, 2:] + padded[:, :, 1:-1, :-2]
    return beside


def emission_weights(chain_all, gamma_all, me):
    groups = chain_all.shape[0]
    g = jnp.arange(groups)[:, None]
    k = jnp.arange(groups)[None, :]
    live = (k > me) & (k <= g)
    factors = jnp.where(live[:, :, None], chain_all[None, :, :], 1.0)
    spread = jnp.prod(factors, axis=1)
    return jnp.where(g >= me, gamma_all * spread, 0.0)


def body(
    density,
    space_factor,
    diff_rate,
    loss_inverse,
    chain_yield,
    survival,
    gamma_yield,
    sky_weight,
    sky_blocks,
):
    tiles = lax.axis_size("space")
    rows = NB // tiles
    params = jnp.stack([chain_yield[0], gamma_yield[0]])
    params_all = lax.all_gather(params, "species")
    blocks_all = lax.all_gather(sky_blocks[0].astype(jnp.float32), "space")
    field = density[0]
    bins = field.shape[0]
    width = field.shape[1]
    depth = field.shape[3]
    rate = diff_rate[0][:, None, None, None]
    factor = rate * space_factor[None]
    for step in range(SUBSTEPS):
        wider = padded_2(field, (("space", 1),), 1)
        beside = wider[:, 2:] + wider[:, :-2] + cross_sum(field)
        field = field + factor * (beside - 6.0 * field)
    solved = jnp.dot(
        loss_inverse[0], field.reshape(bins, -1), precision=HIGH, preferred_element_type=jnp.float32
    ).reshape(field.shape)
    factor_chain = chain_yield[0][:, None, None, None]
    own_part = survival[0][:, None, None, None] * solved
    me = lax.axis_index("species")
    weights = emission_weights(params_all[:, 0], params_all[:, 1], me)
    own_columns = jnp.sum(own_part, axis=3).reshape(bins, -1)
    partial = jnp.dot(weights, own_columns, precision=HIGH, preferred_element_type=jnp.float32)
    sums = lax.psum(partial, "species")
    emission = (sums / (bins * depth)).astype(jnp.bfloat16).astype(jnp.float32)
    columns = jnp.sum(emission, axis=0)
    contribution = jnp.einsum(
        "c,lcb->lb", columns, sky_weight[0].astype(jnp.float32), precision=HIGH
    )
    gathered = lax.all_gather(contribution, "space")
    lines = gathered.shape[1]
    mine = lax.axis_index("space") * rows + jnp.arange(rows, dtype=jnp.int32)
    onehot = (blocks_all.reshape(1, tiles * lines) == mine.astype(jnp.float32)[:, None]).astype(
        jnp.float32
    )
    sky = jnp.dot(
        onehot,
        gathered.reshape(tiles * lines, -1),
        precision=HIGH,
        preferred_element_type=jnp.float32,
    )
    carried = own_part
    for section in range(lax.axis_size("species") - 1):
        carried = factor_chain * from_behind(carried, "species", 1) + own_part
    return (carried[None], sky)


def solution(mesh):
    placed = (
        P("species", None, "space", None, None),
        P("space", None, None),
        P("species", None),
        P("species", None, None),
        P("species", None),
        P("species", None),
        P("species", None),
        P("space", None, None, None),
        P("space", None),
    )
    return jax.shard_map(
        body,
        mesh=mesh,
        in_specs=placed,
        out_specs=(P("species", None, "space", None, None), P("space", None)),
        check_vma=False,
    )
```

profile of v0, /device:TPU:0, one launch (start us, length us, event | category | flops | bytes accessed | tf_op | source)
XLA Modules:
  0.0 139.3 jit_solution(8967124272913731241)
XLA Ops:
  0.7 1.4 fusion.34
  2.0 1.3 collective-permute-start
  3.4 3.1 %collective-permute-start.1 = (f32[32,1,32,128]{3,2,1,0:T(8,128)S(1)}, f32[32,1,32,128]{3,2,1,0:T(8,128)S(1)}, u32[]{:S(2)}, u32[]{:S(2)}) collective-permute-start(f32[32,1,32,128]{3,2,1,0:T(8,128)S(1)} %get-tuple-element.7), channel_id=1, source_target_pairs={{0,1},{1,2},{2,3},{3,4},{4,5},{5,6},{6,7},{8,9},{9,10},{10,11},{11... | collective-permute-start | bytes 1572872 | tf_op jit(solution)/shard_map/ppermute | solution.py:19
  6.4 1.5 %collective-permute-done.1 = f32[32,1,32,128]{3,2,1,0:T(8,128)S(1)} collective-permute-done((f32[32,1,32,128]{3,2,1,0:T(8,128)S(1)}, f32[32,1,32,128]{3,2,1,0:T(8,128)S(1)}, u32[]{:S(2)}, u32[]{:S(2)}) %collective-permute-start.1) | collective-permute-done | bytes 524320 | tf_op jit(solution)/shard_map/ppermute | solution.py:19
  7.9 0.8 fusion
  8.8 1.3 collective-permute-start.2
  10.1 10.4 %collective-permute-start.3 = (f32[32,1,32,128]{3,2,1,0:T(8,128)S(1)}, f32[32,1,32,128]{3,2,1,0:T(8,128)S(1)}, u32[]{:S(2)}, u32[]{:S(2)}) collective-permute-start(f32[32,1,32,128]{3,2,1,0:T(8,128)S(1)} %get-tuple-element.5), channel_id=1, source_target_pairs={{0,1},{1,2},{2,3},{3,4},{4,5},{5,6},{6,7},{8,9},{9,10},{10,11},{11... | collective-permute-start | bytes 1572872 | tf_op jit(solution)/shard_map/ppermute | solution.py:19
  20.5 1.5 %collective-permute-done.3 = f32[32,1,32,128]{3,2,1,0:T(8,128)S(1)} collective-permute-done((f32[32,1,32,128]{3,2,1,0:T(8,128)S(1)}, f32[32,1,32,128]{3,2,1,0:T(8,128)S(1)}, u32[]{:S(2)}, u32[]{:S(2)}) %collective-permute-start.3) | collective-permute-done | bytes 524320 | tf_op jit(solution)/shard_map/ppermute | solution.py:19
  22.0 0.8 fusion.1
  22.8 1.7 %convolution_bitcast_fusion = f32[4,8,64,128]{3,1,2,0:T(8,128)S(1)} fusion(f32[4,8,64,128]{3,2,1,0:T(8,128)S(1)} %bitcast.49, f32[1,32,32]{2,1,0:T(8,128)S(1)} %copy-done.3), kind=kOutput, calls=%fused_computation.10 | convolution fusion | flops 100663296 | bytes 2101248 | tf_op jit(solution)/shard_map/dot_general | solution.py:77
  24.5 0.2 copy.17
  24.7 0.5 copy-done.6
  25.2 0.5 fusion.32
  25.7 3.6 %collective-permute-start.4 = (f32[32,2,32,128]{3,2,1,0:T(8,128)S(1)}, f32[32,2,32,128]{3,2,1,0:T(8,128)S(1)}, u32[]{:S(2)}, u32[]{:S(2)}) collective-permute-start(f32[32,2,32,128]{3,2,1,0:T(8,128)S(1)} %get-tuple-element.3), channel_id=1, source_target_pairs={{0,8},{8,16},{16,24},{1,9},{9,17},{17,25},{2,10},{10,18},{18,26},{... | collective-permute-start | bytes 3145736 | tf_op jit(solution)/shard_map/ppermute | solution.py:31
  29.2 18.0 %collective-permute-done.4 = f32[32,2,32,128]{3,2,1,0:T(8,128)S(1)} collective-permute-done((f32[32,2,32,128]{3,2,1,0:T(8,128)S(1)}, f32[32,2,32,128]{3,2,1,0:T(8,128)S(1)}, u32[]{:S(2)}, u32[]{:S(2)}) %collective-permute-start.4) | collective-permute-done | bytes 1048608 | tf_op jit(solution)/shard_map/ppermute | solution.py:31
  47.2 0.2 multiply_add_fusion.1
  47.5 5.4 %collective-permute-start.5 = (f32[32,2,32,128]{3,2,1,0:T(8,128)S(1)}, f32[32,2,32,128]{3,2,1,0:T(8,128)}, u32[]{:S(2)}, u32[]{:S(2)}) collective-permute-start(f32[32,2,32,128]{3,2,1,0:T(8,128)S(1)} %multiply_add_fusion.1), channel_id=1, source_target_pairs={{0,8},{8,16},{16,24},{1,9},{9,17},{17,25},{2,10},{10,18},{18,26},{... | collective-permute-start | bytes 3145736 | tf_op jit(solution)/shard_map/ppermute | solution.py:31
  52.8 24.3 %all-gather.3 = f32[4,2,32]{2,1,0:T(2,128)S(1)} all-gather(f32[1,2,32]{2,1,0:T(2,128)S(1)} %maximum_bitcast_fusion), channel_id=2, replica_groups=mesh['species'=4,'space'=8] {'species'}, dimensions={0}, use_global_device_ids=true | all-gather | bytes 1280 | tf_op jit(solution)/shard_map/all_gather | solution.py:65
  77.2 1.4 multiply_add_fusion
  78.6 1.4 collective-permute-start.6
  80.0 29.6 %all-gather.2 = f32[8,1,8]{2,1,0:T(1,128)S(1)} all-gather(f32[1,1,8]{2,1,0:T(1,128)S(1)} %convert_bitcast_fusion), channel_id=1, replica_groups=mesh['species'=4,'space'=8] {'space'}, dimensions={0}, use_global_device_ids=true | all-gather | bytes 288 | tf_op jit(solution)/shard_map/all_gather | solution.py:66
  109.6 0.5 broadcast.46
  110.1 0.7 reduce.3
  110.8 0.1 eq.15
  110.9 0.1 select_reduce_fusion
  111.0 0.1 reshape.73
  111.0 0.2 fusion.23
  111.2 8.9 %psum.7 = f32[4,64]{1,0:T(4,128)S(1)} all-reduce(f32[4,64]{1,0:T(4,128)S(1)} %fusion.23), channel_id=1, replica_groups=mesh['species'=4,'space'=8] {'species'}, use_global_device_ids=true, to_apply=%region_2.3 | all-reduce | flops 256 | bytes 2048 | tf_op jit(solution)/shard_map/psum | solution.py:86
  120.2 0.2 fusion.16
  120.3 17.1 %all-gather.1 = f32[64,128]{1,0:T(8,128)S(1)} all-gather(f32[8,128]{1,0:T(8,128)S(1)} %bitcast.50), channel_id=3, replica_groups=mesh['species'=4,'space'=8] {'space'}, dimensions={0}, use_global_device_ids=true | all-gather | bytes 36864 | tf_op jit(solution)/shard_map/all_gather | solution.py:92
  137.4 0.8 fusion.18
  138.2 1.1 add_bitcast_fusion
  (30 shorter events, 0.2 us)
Async XLA Ops:
  0.6 119.5 %copy-start = (bf16[1,8,64,128]{3,2,1,0:T(8,128)(2,1)S(1)}, bf16[1,8,64,128]{3,2,1,0:T(8,128)(2,1)}, u32[]{:S(2)}) copy-start(bf16[1,8,64,128]{3,2,1,0:T(8,128)(2,1)} %param.16) | copy-start | bytes 393220
  0.6 7.3 %copy-start.1 = (f32[1,32,2,32,128]{4,3,2,1,0:T(8,128)S(1)}, f32[1,32,2,32,128]{4,3,2,1,0:T(8,128)}, u32[]{:S(2)}) copy-start(f32[1,32,2,32,128]{4,3,2,1,0:T(8,128)} %param.9) | copy-start | bytes 3145732
  0.7 7.3 %copy-start.2 = (f32[2,32,128]{2,1,0:T(8,128)S(1)}, f32[2,32,128]{2,1,0:T(8,128)}, u32[]{:S(2)}) copy-start(f32[2,32,128]{2,1,0:T(8,128)} %param.10) | copy-start | bytes 98308
  0.7 7.2 %copy-start.5 = (f32[1,32]{1,0:T(1,128)S(1)}, f32[1,32]{1,0:T(1,128)}, u32[]{:S(2)}) copy-start(f32[1,32]{1,0:T(1,128)} %param.11) | copy-start | bytes 388
  2.0 4.4 %collective-permute-start = (f32[32,1,32,128]{3,2,1,0:T(8,128)S(1)}, f32[32,1,32,128]{3,2,1,0:T(8,128)S(1)}, u32[]{:S(2)}, u32[]{:S(2)}) collective-permute-start(f32[32,1,32,128]{3,2,1,0:T(8,128)S(1)} %get-tuple-element.6), channel_id=1, source_target_pairs={{1,0},{2,1},{3,2},{4,3},{5,4},{6,5},{7,6},{9,8},{10,9},{11,10},{12... | collective-permute-start | bytes 1572872 | tf_op jit(solution)/shard_map/ppermute | solution.py:21
  3.4 4.6 %collective-permute-start.1 = (f32[32,1,32,128]{3,2,1,0:T(8,128)S(1)}, f32[32,1,32,128]{3,2,1,0:T(8,128)S(1)}, u32[]{:S(2)}, u32[]{:S(2)}) collective-permute-start(f32[32,1,32,128]{3,2,1,0:T(8,128)S(1)} %get-tuple-element.7), channel_id=1, source_target_pairs={{0,1},{1,2},{2,3},{3,4},{4,5},{5,6},{6,7},{8,9},{9,10},{10,11},{11... | collective-permute-start | bytes 1572872 | tf_op jit(solution)/shard_map/ppermute | solution.py:19
  8.8 11.7 %collective-permute-start.2 = (f32[32,1,32,128]{3,2,1,0:T(8,128)S(1)}, f32[32,1,32,128]{3,2,1,0:T(8,128)S(1)}, u32[]{:S(2)}, u32[]{:S(2)}) collective-permute-start(f32[32,1,32,128]{3,2,1,0:T(8,128)S(1)} %get-tuple-element.4), channel_id=1, source_target_pairs={{1,0},{2,1},{3,2},{4,3},{5,4},{6,5},{7,6},{9,8},{10,9},{11,10},{12... | collective-permute-start | bytes 1572872 | tf_op jit(solution)/shard_map/ppermute | solution.py:21
  10.1 12.7 %copy-start.3 = (f32[1,32,32]{2,1,0:T(8,128)S(1)}, f32[1,32,32]{2,1,0:T(8,128)}, u32[]{:S(2)}) copy-start(f32[1,32,32]{2,1,0:T(8,128)} %param.12) | copy-start | bytes 12292
  10.1 11.9 %collective-permute-start.3 = (f32[32,1,32,128]{3,2,1,0:T(8,128)S(1)}, f32[32,1,32,128]{3,2,1,0:T(8,128)S(1)}, u32[]{:S(2)}, u32[]{:S(2)}) collective-permute-start(f32[32,1,32,128]{3,2,1,0:T(8,128)S(1)} %get-tuple-element.5), channel_id=1, source_target_pairs={{0,1},{1,2},{2,3},{3,4},{4,5},{5,6},{6,7},{8,9},{9,10},{10,11},{11... | collective-permute-start | bytes 1572872 | tf_op jit(solution)/shard_map/ppermute | solution.py:19
  24.5 0.7 copy-start.6
  25.2 22.0 %copy-start.4 = (f32[1,32]{1,0:T(1,128)S(1)}, f32[1,32]{1,0:T(1,128)}, u32[]{:S(2)}) copy-start(f32[1,32]{1,0:T(1,128)} %param.13) | copy-start | bytes 388
  25.7 21.5 %collective-permute-start.4 = (f32[32,2,32,128]{3,2,1,0:T(8,128)S(1)}, f32[32,2,32,128]{3,2,1,0:T(8,128)S(1)}, u32[]{:S(2)}, u32[]{:S(2)}) collective-permute-start(f32[32,2,32,128]{3,2,1,0:T(8,128)S(1)} %get-tuple-element.3), channel_id=1, source_target_pairs={{0,8},{8,16},{16,24},{1,9},{9,17},{17,25},{2,10},{10,18},{18,26},{... | collective-permute-start | bytes 3145736 | tf_op jit(solution)/shard_map/ppermute | solution.py:31
  47.2 5.6 %copy-start.7 = (f32[1,32]{1,0:T(1,128)S(1)}, f32[1,32]{1,0:T(1,128)}, u32[]{:S(2)}) copy-start(f32[1,32]{1,0:T(1,128)} %param.15) | copy-start | bytes 388
  47.2 30.0 %copy-start.8 = (s32[1,8]{1,0:T(1,128)S(1)}, s32[1,8]{1,0:T(1,128)}, u32[]{:S(2)}) copy-start(s32[1,8]{1,0:T(1,128)} %param.17) | copy-start | bytes 100
  47.5 29.7 %collective-permute-start.5 = (f32[32,2,32,128]{3,2,1,0:T(8,128)S(1)}, f32[32,2,32,128]{3,2,1,0:T(8,128)}, u32[]{:S(2)}, u32[]{:S(2)}) collective-permute-start(f32[32,2,32,128]{3,2,1,0:T(8,128)S(1)} %multiply_add_fusion.1), channel_id=1, source_target_pairs={{0,8},{8,16},{16,24},{1,9},{9,17},{17,25},{2,10},{10,18},{18,26},{... | collective-permute-start | bytes 3145736 | tf_op jit(solution)/shard_map/ppermute | solution.py:31
  78.6 59.6 %collective-permute-start.6 = (f32[32,2,32,128]{3,2,1,0:T(8,128)S(1)}, f32[32,2,32,128]{3,2,1,0:T(8,128)S(1)}, u32[]{:S(2)}, u32[]{:S(2)}) collective-permute-start(f32[32,2,32,128]{3,2,1,0:T(8,128)S(1)} %multiply_add_fusion), channel_id=1, source_target_pairs={{0,8},{8,16},{16,24},{1,9},{9,17},{17,25},{2,10},{10,18},{18,26},{... | collective-permute-start | bytes 3145736 | tf_op jit(solution)/shard_map/ppermute | solution.py:31
where the time goes:
time: 140 us; the launch traced here: 139 us
  blocking collectives  79.9 us (57%)
  starting transfers between devices  26.3 us (19%)
  waiting for transfers between devices  20.9 us (15%)
  other arithmetic  5.66 us (4%)
  matrix products  2.84 us (2%)
  local copies, waits for them, and re-layouts  2.81 us (2%)
    all_gather x1, blocking collectives, body(): blocks_all = lax.all_gather(sky_blocks[0].astype(jnp.float32), 'space')  29.6 us
    all_gather x1, blocking collectives, body(): params_all = lax.all_gather(params, 'species')  24.3 us
    ppermute x3, waiting for transfers between devices, from_behind(): return lax.ppermute(block, axis, route)  18 us
    all_gather x1, blocking collectives, body(): gathered = lax.all_gather(contribution, 'space')  17.1 us
    ppermute x2, starting transfers between devices, padded_2(): lax.ppermute(tail, axis, [(i, (i + 1) % count) for i in range(ends)])  13.5 us
    ppermute x3, starting transfers between devices, from_behind(): return lax.ppermute(block, axis, route)  10.3 us
    psum x1, blocking collectives, body(): sums = lax.psum(partial, 'species')  8.89 us
    ppermute x2, waiting for transfers between devices, padded_2(): lax.ppermute(tail, axis, [(i, (i + 1) % count) for i in range(ends)])  2.95 us
  transfers between devices with their start and end apart: 7, of which 3 were waited for; matrix products, arithmetic and copies ran while one was open for 2% of the time, Pallas kernels for 0%

commit v1 on v0

--- a/solution.py
+++ b/solution.py
@@ -83,7 +83,7 @@
     weights = emission_weights(params_all[:, 0], params_all[:, 1], me)
     own_columns = jnp.sum(own_part, axis=3).reshape(bins, -1)
     partial = jnp.dot(weights, own_columns, precision=HIGH, preferred_element_type=jnp.float32)
-    sums = lax.psum(partial, "species")
+    sums = jnp.sum(lax.all_gather(partial, "species"), axis=0)
     emission = (sums / (bins * depth)).astype(jnp.bfloat16).astype(jnp.float32)
     columns = jnp.sum(emission, axis=0)
     contribution = jnp.einsum(

time: 140 us -> 150 us (1.071)
  waiting for transfers between devices: 20.9 us -> 39 us
  blocking collectives: 79.9 us -> 68.4 us
  starting transfers between devices: 26.3 us -> 29.5 us
    ppermute x3, waiting for transfers between devices: 18 us -> 36.1 us  [from_behind(): return lax.ppermute(block, axis, route)]
    all_gather x1, blocking collectives: 24.3 us -> 9.08 us  [body(): params_all = lax.all_gather(params, 'species')]
    all_gather x0 -> x1, blocking collectives: none -> 11.9 us  [body(): sums = jnp.sum(lax.all_gather(partial, 'species'), axis=0)]
    psum x1 -> x0, blocking collectives: 8.89 us -> none  [body(): sums = lax.psum(partial, 'species')]
    ppermute x3, starting transfers between devices: 10.3 us -> 13.5 us  [from_behind(): return lax.ppermute(block, axis, route)]
  transfers between devices with their start and end apart: 7 -> 7, of which waited for: 3 -> 4; matrix products, arithmetic and copies ran while one was open for 2% -> 2% of each run, Pallas kernels for 0% -> 0%
where the time goes in v1:
time: 150 us; the launch traced here: 149 us
  blocking collectives  68.4 us (46%)
  waiting for transfers between devices  39 us (26%)
  starting transfers between devices  29.5 us (20%)
  other arithmetic  5.68 us (4%)
  matrix products  2.84 us (2%)
  local copies, waits for them, and re-layouts  2.81 us (2%)
    ppermute x3, waiting for transfers between devices, from_behind(): return lax.ppermute(block, axis, route)  36.1 us
    all_gather x1, blocking collectives, body(): blocks_all = lax.all_gather(sky_blocks[0].astype(jnp.float32), 'space')  29.6 us
    all_gather x1, blocking collectives, body(): gathered = lax.all_gather(contribution, 'space')  17.9 us
    ppermute x3, starting transfers between devices, from_behind(): return lax.ppermute(block, axis, route)  13.5 us
    ppermute x2, starting transfers between devices, padded_2(): lax.ppermute(tail, axis, [(i, (i + 1) % count) for i in range(ends)])  13.5 us
    all_gather x1, blocking collectives, body(): sums = jnp.sum(lax.all_gather(partial, 'species'), axis=0)  11.9 us
    all_gather x1, blocking collectives, body(): params_all = lax.all_gather(params, 'species')  9.08 us
  transfers between devices with their start and end apart: 7, of which 4 were waited for; matrix products, arithmetic and copies ran while one was open for 2% of the time, Pallas kernels for 0%

profile of v1, /device:TPU:0, one launch (start us, length us, event | category | flops | bytes accessed | tf_op | source)
XLA Modules:
  0.0 149.2 jit_solution(12276237256506663535)
XLA Ops:
  0.7 1.4 fusion.33
  2.0 1.3 collective-permute-start
  3.4 3.1 %collective-permute-start.1 = (f32[32,1,32,128]{3,2,1,0:T(8,128)S(1)}, f32[32,1,32,128]{3,2,1,0:T(8,128)S(1)}, u32[]{:S(2)}, u32[]{:S(2)}) collective-permute-start(f32[32,1,32,128]{3,2,1,0:T(8,128)S(1)} %get-tuple-element.7), channel_id=1, source_target_pairs={{0,1},{1,2},{2,3},{3,4},{4,5},{5,6},{6,7},{8,9},{9,10},{10,11},{11... | collective-permute-start | bytes 1572872 | tf_op jit(solution)/shard_map/ppermute | solution.py:19
  6.4 1.5 collective-permute-done.1
  7.9 0.8 fusion
  8.8 1.3 collective-permute-start.2
  10.1 10.4 %collective-permute-start.3 = (f32[32,1,32,128]{3,2,1,0:T(8,128)S(1)}, f32[32,1,32,128]{3,2,1,0:T(8,128)S(1)}, u32[]{:S(2)}, u32[]{:S(2)}) collective-permute-start(f32[32,1,32,128]{3,2,1,0:T(8,128)S(1)} %get-tuple-element.5), channel_id=1, source_target_pairs={{0,1},{1,2},{2,3},{3,4},{4,5},{5,6},{6,7},{8,9},{9,10},{10,11},{11... | collective-permute-start | bytes 1572872 | tf_op jit(solution)/shard_map/ppermute | solution.py:19
  20.5 1.5 collective-permute-done.3
  22.0 0.8 fusion.1
  22.8 1.7 %convolution_bitcast_fusion = f32[4,8,64,128]{3,1,2,0:T(8,128)S(1)} fusion(f32[4,8,64,128]{3,2,1,0:T(8,128)S(1)} %bitcast.51, f32[1,32,32]{2,1,0:T(8,128)S(1)} %copy-done.3), kind=kOutput, calls=%fused_computation.10 | convolution fusion | flops 100663296 | bytes 2101248 | tf_op jit(solution)/shard_map/dot_general | solution.py:77
  24.5 0.2 copy.17
  24.7 0.5 copy-done.6
  25.2 0.5 fusion.31
  25.7 3.6 %collective-permute-start.4 = (f32[32,2,32,128]{3,2,1,0:T(8,128)S(1)}, f32[32,2,32,128]{3,2,1,0:T(8,128)S(1)}, u32[]{:S(2)}, u32[]{:S(2)}) collective-permute-start(f32[32,2,32,128]{3,2,1,0:T(8,128)S(1)} %get-tuple-element.3), channel_id=1, source_target_pairs={{0,8},{8,16},{16,24},{1,9},{9,17},{17,25},{2,10},{10,18},{18,26},{... | collective-permute-start | bytes 3145736 | tf_op jit(solution)/shard_map/ppermute | solution.py:31
  29.2 18.0 %collective-permute-done.4 = f32[32,2,32,128]{3,2,1,0:T(8,128)S(1)} collective-permute-done((f32[32,2,32,128]{3,2,1,0:T(8,128)S(1)}, f32[32,2,32,128]{3,2,1,0:T(8,128)S(1)}, u32[]{:S(2)}, u32[]{:S(2)}) %collective-permute-start.4) | collective-permute-done | bytes 1048608 | tf_op jit(solution)/shard_map/ppermute | solution.py:31
  47.2 0.2 multiply_add_fusion.1
  47.5 5.4 %collective-permute-start.5 = (f32[32,2,32,128]{3,2,1,0:T(8,128)S(1)}, f32[32,2,32,128]{3,2,1,0:T(8,128)}, u32[]{:S(2)}, u32[]{:S(2)}) collective-permute-start(f32[32,2,32,128]{3,2,1,0:T(8,128)S(1)} %multiply_add_fusion.1), channel_id=1, source_target_pairs={{0,8},{8,16},{16,24},{1,9},{9,17},{17,25},{2,10},{10,18},{18,26},{... | collective-permute-start | bytes 3145736 | tf_op jit(solution)/shard_map/ppermute | solution.py:31
  52.9 18.1 %collective-permute-done.5 = f32[32,2,32,128]{3,2,1,0:T(8,128)} collective-permute-done((f32[32,2,32,128]{3,2,1,0:T(8,128)S(1)}, f32[32,2,32,128]{3,2,1,0:T(8,128)}, u32[]{:S(2)}, u32[]{:S(2)}) %collective-permute-start.5) | collective-permute-done | bytes 1048608 | tf_op jit(solution)/shard_map/ppermute | solution.py:31
  71.0 1.4 multiply_add_fusion
  72.4 4.6 %collective-permute-start.6 = (f32[32,2,32,128]{3,2,1,0:T(8,128)S(1)}, f32[32,2,32,128]{3,2,1,0:T(8,128)S(1)}, u32[]{:S(2)}, u32[]{:S(2)}) collective-permute-start(f32[32,2,32,128]{3,2,1,0:T(8,128)S(1)} %multiply_add_fusion), channel_id=1, source_target_pairs={{0,8},{8,16},{16,24},{1,9},{9,17},{17,25},{2,10},{10,18},{18,26},{... | collective-permute-start | bytes 3145736 | tf_op jit(solution)/shard_map/ppermute | solution.py:31
  77.0 29.6 %all-gather.3 = f32[8,1,8]{2,1,0:T(1,128)S(1)} all-gather(f32[1,1,8]{2,1,0:T(1,128)S(1)} %convert_bitcast_fusion), channel_id=1, replica_groups=mesh['species'=4,'space'=8] {'space'}, dimensions={0}, use_global_device_ids=true | all-gather | bytes 288 | tf_op jit(solution)/shard_map/all_gather | solution.py:66
  106.6 0.5 broadcast.46
  107.1 0.7 reduce.4
  107.8 9.1 %all-gather.4 = f32[4,2,32]{2,1,0:T(2,128)S(1)} all-gather(f32[1,2,32]{2,1,0:T(2,128)S(1)} %maximum_bitcast_fusion), channel_id=2, replica_groups=mesh['species'=4,'space'=8] {'species'}, dimensions={0}, use_global_device_ids=true | all-gather | bytes 1280 | tf_op jit(solution)/shard_map/all_gather | solution.py:65
  116.9 0.1 select_reduce_fusion
  117.0 0.1 reshape.73
  117.1 0.2 convolution_bitcast_fusion.1
  117.3 11.9 %all-gather.5 = f32[4,4,64]{2,1,0:T(4,128)S(1)} all-gather(f32[1,4,64]{2,1,0:T(4,128)S(1)} %convolution_bitcast_fusion.1), channel_id=3, replica_groups=mesh['species'=4,'space'=8] {'species'}, dimensions={0}, use_global_device_ids=true | all-gather | bytes 5120 | tf_op jit(solution)/shard_map/all_gather | solution.py:86
  129.2 0.2 fusion.16
  129.3 17.9 %all-gather.2 = f32[64,128]{1,0:T(8,128)S(1)} all-gather(f32[8,128]{1,0:T(8,128)S(1)} %bitcast.52), channel_id=4, replica_groups=mesh['species'=4,'space'=8] {'space'}, dimensions={0}, use_global_device_ids=true | all-gather | bytes 36864 | tf_op jit(solution)/shard_map/all_gather | solution.py:92
  147.2 0.8 fusion.18
  148.0 1.1 add_bitcast_fusion
  (31 shorter events, 0.3 us)
Async XLA Ops:
  0.6 128.6 %copy-start = (bf16[1,8,64,128]{3,2,1,0:T(8,128)(2,1)S(1)}, bf16[1,8,64,128]{3,2,1,0:T(8,128)(2,1)}, u32[]{:S(2)}) copy-start(bf16[1,8,64,128]{3,2,1,0:T(8,128)(2,1)} %param.16) | copy-start | bytes 393220
  0.6 7.3 %copy-start.1 = (f32[1,32,2,32,128]{4,3,2,1,0:T(8,128)S(1)}, f32[1,32,2,32,128]{4,3,2,1,0:T(8,128)}, u32[]{:S(2)}) copy-start(f32[1,32,2,32,128]{4,3,2,1,0:T(8,128)} %param.9) | copy-start | bytes 3145732
  0.7 7.3 %copy-start.2 = (f32[2,32,128]{2,1,0:T(8,128)S(1)}, f32[2,32,128]{2,1,0:T(8,128)}, u32[]{:S(2)}) copy-start(f32[2,32,128]{2,1,0:T(8,128)} %param.10) | copy-start | bytes 98308
  0.7 7.2 %copy-start.5 = (f32[1,32]{1,0:T(1,128)S(1)}, f32[1,32]{1,0:T(1,128)}, u32[]{:S(2)}) copy-start(f32[1,32]{1,0:T(1,128)} %param.11) | copy-start | bytes 388
  2.0 4.4 %collective-permute-start = (f32[32,1,32,128]{3,2,1,0:T(8,128)S(1)}, f32[32,1,32,128]{3,2,1,0:T(8,128)S(1)}, u32[]{:S(2)}, u32[]{:S(2)}) collective-permute-start(f32[32,1,32,128]{3,2,1,0:T(8,128)S(1)} %get-tuple-element.6), channel_id=1, source_target_pairs={{1,0},{2,1},{3,2},{4,3},{5,4},{6,5},{7,6},{9,8},{10,9},{11,10},{12... | collective-permute-start | bytes 1572872 | tf_op jit(solution)/shard_map/ppermute | solution.py:21
  3.4 4.6 %collective-permute-start.1 = (f32[32,1,32,128]{3,2,1,0:T(8,128)S(1)}, f32[32,1,32,128]{3,2,1,0:T(8,128)S(1)}, u32[]{:S(2)}, u32[]{:S(2)}) collective-permute-start(f32[32,1,32,128]{3,2,1,0:T(8,128)S(1)} %get-tuple-element.7), channel_id=1, source_target_pairs={{0,1},{1,2},{2,3},{3,4},{4,5},{5,6},{6,7},{8,9},{9,10},{10,11},{11... | collective-permute-start | bytes 1572872 | tf_op jit(solution)/shard_map/ppermute | solution.py:19
  8.8 11.7 %collective-permute-start.2 = (f32[32,1,32,128]{3,2,1,0:T(8,128)S(1)}, f32[32,1,32,128]{3,2,1,0:T(8,128)S(1)}, u32[]{:S(2)}, u32[]{:S(2)}) collective-permute-start(f32[32,1,32,128]{3,2,1,0:T(8,128)S(1)} %get-tuple-element.4), channel_id=1, source_target_pairs={{1,0},{2,1},{3,2},{4,3},{5,4},{6,5},{7,6},{9,8},{10,9},{11,10},{12... | collective-permute-start | bytes 1572872 | tf_op jit(solution)/shard_map/ppermute | solution.py:21
  10.1 12.7 %copy-start.3 = (f32[1,32,32]{2,1,0:T(8,128)S(1)}, f32[1,32,32]{2,1,0:T(8,128)}, u32[]{:S(2)}) copy-start(f32[1,32,32]{2,1,0:T(8,128)} %param.12) | copy-start | bytes 12292
  10.1 11.9 %collective-permute-start.3 = (f32[32,1,32,128]{3,2,1,0:T(8,128)S(1)}, f32[32,1,32,128]{3,2,1,0:T(8,128)S(1)}, u32[]{:S(2)}, u32[]{:S(2)}) collective-permute-start(f32[32,1,32,128]{3,2,1,0:T(8,128)S(1)} %get-tuple-element.5), channel_id=1, source_target_pairs={{0,1},{1,2},{2,3},{3,4},{4,5},{5,6},{6,7},{8,9},{9,10},{10,11},{11... | collective-permute-start | bytes 1572872 | tf_op jit(solution)/shard_map/ppermute | solution.py:19
  24.5 0.7 copy-start.6
  25.2 22.0 %copy-start.4 = (f32[1,32]{1,0:T(1,128)S(1)}, f32[1,32]{1,0:T(1,128)}, u32[]{:S(2)}) copy-start(f32[1,32]{1,0:T(1,128)} %param.13) | copy-start | bytes 388
  25.7 21.5 %collective-permute-start.4 = (f32[32,2,32,128]{3,2,1,0:T(8,128)S(1)}, f32[32,2,32,128]{3,2,1,0:T(8,128)S(1)}, u32[]{:S(2)}, u32[]{:S(2)}) collective-permute-start(f32[32,2,32,128]{3,2,1,0:T(8,128)S(1)} %get-tuple-element.3), channel_id=1, source_target_pairs={{0,8},{8,16},{16,24},{1,9},{9,17},{17,25},{2,10},{10,18},{18,26},{... | collective-permute-start | bytes 3145736 | tf_op jit(solution)/shard_map/ppermute | solution.py:31
  47.2 5.6 %copy-start.7 = (f32[1,32]{1,0:T(1,128)S(1)}, f32[1,32]{1,0:T(1,128)}, u32[]{:S(2)}) copy-start(f32[1,32]{1,0:T(1,128)} %param.15) | copy-start | bytes 388
  47.2 5.7 %copy-start.8 = (s32[1,8]{1,0:T(1,128)S(1)}, s32[1,8]{1,0:T(1,128)}, u32[]{:S(2)}) copy-start(s32[1,8]{1,0:T(1,128)} %param.17) | copy-start | bytes 100
  47.5 23.5 %collective-permute-start.5 = (f32[32,2,32,128]{3,2,1,0:T(8,128)S(1)}, f32[32,2,32,128]{3,2,1,0:T(8,128)}, u32[]{:S(2)}, u32[]{:S(2)}) collective-permute-start(f32[32,2,32,128]{3,2,1,0:T(8,128)S(1)} %multiply_add_fusion.1), channel_id=1, source_target_pairs={{0,8},{8,16},{16,24},{1,9},{9,17},{17,25},{2,10},{10,18},{18,26},{... | collective-permute-start | bytes 3145736 | tf_op jit(solution)/shard_map/ppermute | solution.py:31
  72.4 75.7 %collective-permute-start.6 = (f32[32,2,32,128]{3,2,1,0:T(8,128)S(1)}, f32[32,2,32,128]{3,2,1,0:T(8,128)S(1)}, u32[]{:S(2)}, u32[]{:S(2)}) collective-permute-start(f32[32,2,32,128]{3,2,1,0:T(8,128)S(1)} %multiply_add_fusion), channel_id=1, source_target_pairs={{0,8},{8,16},{16,24},{1,9},{9,17},{17,25},{2,10},{10,18},{18,26},{... | collective-permute-start | bytes 3145736 | tf_op jit(solution)/shard_map/ppermute | solution.py:31
